TPU v7x, 512 devices: a whole 4x8x8 slice. The times are simulated.
512 devices in a mesh: gz: 64 (over x, z, y_lo), gx: 8 (over y_hi, core).
Axes of the slice: x: 4, y: 8 (y_hi: 4, y_lo: 2; y = y_hi * 2 + y_lo), z: 8, core: 2. Of those that a mesh axis runs over, the one named last changes fastest.
Arguments:
- latent: float32 [8, 128, 32, 128], P(None, 'gz', 'gx'), may hold values from -6 to 6
- condition: bfloat16 [8, 128, 32, 128], P(None, 'gz', 'gx'), may hold values from -6 to 6
- cotangent: float32 [8, 128, 32, 128], P(None, 'gz', 'gx'), may hold values from -6 to 6
- expand_kernel: bfloat16 [27, 64, 12], replicated, may hold values from -0.3125 to 0.3125
- mixing_matrix: bfloat16 [64, 64], replicated, may hold values from -0.75 to 0.75
- project_kernel: bfloat16 [27, 8, 64], replicated, may hold values from -0.15625 to 0.15625
- offsets: float32 [136], replicated, may hold values from -3 to 3
Outputs:
- restored: float32 [256, 64, 256], P('gz', 'gx')
- field_grad: float32 [256, 64, 256], P('gz', 'gx')
- condition_grad: float32 [8, 128, 32, 128], P(None, 'gz', 'gx')
- expand_grad: float32 [27, 64, 12], replicated
- mixing_grad: float32 [64, 64], replicated
- project_grad: float32 [27, 8, 64], replicated
- offset_grad: float32 [136], replicated
All inputs are finite; a program needn't handle non-finite values.
Results may differ from a plain program's by a relative error of at most 0.007.
Values may be sent and summed in bfloat16 or wider, within the bound.
No kernel may reach another device: no remote copies, remote signals or barrier semaphores. Data moves between devices by JAX's collectives and lax.ppermute only.
A program may use at most 64 MiB of HBM per device.

v0:
```python
import math
import jax
import jax.numpy as jnp
import numpy as np
from jax import lax
from jax.sharding import PartitionSpec as P

CH = 4


def extended(cells, sides, width):
    for axis, dim in sides:
        count = lax.axis_size(axis)
        ends = count - 1
        head = lax.slice_in_dim(cells, 0, width, axis=dim)
        tail = lax.slice_in_dim(cells, cells.shape[dim] - width, cells.shape[dim], axis=dim)
        cells = jnp.concatenate(
            [
                lax.ppermute(tail, axis, [(i, (i + 1) % count) for i in range(ends)]),
                cells,
                lax.ppermute(head, axis, [((i + 1) % count, i) for i in range(ends)]),
            ],
            axis=dim,
        )
    return cells


def set_bits(value):
    parity_count = 0
    for bit_place in range(3):
        parity_count = parity_count + (value >> bit_place & 1)
    return parity_count


def haar_table():
    signs = np.zeros((8, 8), np.float32)
    for fine_index in range(8):
        for coef_index in range(8):
            parity = set_bits(fine_index & coef_index)
            signs[fine_index, coef_index] = (-1.0) ** parity / np.sqrt(8.0)
    return signs


def unsqueeze(coarse):
    haar_signs = jnp.asarray(haar_table())
    spread = jnp.einsum("pk,kzxy->pzxy", haar_signs, coarse, precision=lax.Precision.HIGHEST)
    planes, x_rows, y_cols = (coarse.shape[1], coarse.shape[2], coarse.shape[3])
    spread = spread.reshape(2, 2, 2, planes, x_rows, y_cols).transpose(3, 0, 4, 1, 5, 2)
    return spread.reshape(2 * planes, 2 * x_rows, 2 * y_cols)


def silu_slope(preact):
    sigma = jax.nn.sigmoid(preact)
    return sigma * (1.0 + preact * (1.0 - sigma))


def forward_taps(padded, weight, planes, x_rows):
    y_cols = padded.shape[3] - 2
    summed = None
    for tap_index in range(27):
        z_step, x_step, y_step = (tap_index // 9, tap_index // 3 % 3, tap_index % 3)
        sliced = padded[
            :, z_step : z_step + planes, x_step : x_step + x_rows, y_step : y_step + y_cols
        ]
        product = jnp.einsum(
            "oc,czxy->ozxy", weight[tap_index], sliced, preferred_element_type=jnp.float32
        )
        summed = product if summed is None else summed + product
    return summed


def backward_taps(padded, weight, planes, x_rows):
    y_cols = padded.shape[3] - 2
    summed = None
    for tap_index in range(27):
        z_step, x_step, y_step = (tap_index // 9, tap_index // 3 % 3, tap_index % 3)
        sliced = padded[
            :,
            2 - z_step : 2 - z_step + planes,
            2 - x_step : 2 - x_step + x_rows,
            2 - y_step : 2 - y_step + y_cols,
        ]
        product = jnp.einsum(
            "oc,ozxy->czxy", weight[tap_index], sliced, preferred_element_type=jnp.float32
        )
        summed = product if summed is None else summed + product
    return summed


def weight_taps(grad, padded):
    planes, x_rows, y_cols = (grad.shape[1], grad.shape[2], grad.shape[3])
    result = []
    for tap_index in range(27):
        z_step, x_step, y_step = (tap_index // 9, tap_index // 3 % 3, tap_index % 3)
        sliced = padded[
            :, z_step : z_step + planes, x_step : x_step + x_rows, y_step : y_step + y_cols
        ]
        result.append(jnp.einsum("ozxy,czxy->oc", grad, sliced, preferred_element_type=jnp.float32))
    return jnp.stack(result)


def frame_cols(tensor):
    return jnp.pad(tensor, ((0, 0), (0, 0), (0, 0), (1, 1)))


def channel_sums(tensor):
    return jnp.sum(tensor.astype(jnp.float32), axis=(1, 2, 3))


def per_device(latent, condition, cotangent, expand_kernel, mixing_matrix, project_kernel, offsets):
    planes, x_rows, y_cols = (latent.shape[1], latent.shape[2], latent.shape[3])
    hidden_width = mixing_matrix.shape[0]
    upper_half, lower_half = (latent[:CH], latent[CH:])
    cot_upper, cot_lower = (cotangent[:CH], cotangent[CH:])
    expand_offset = offsets[:hidden_width][:, None, None, None]
    mixing_offset = offsets[hidden_width : 2 * hidden_width][:, None, None, None]
    project_offset = offsets[2 * hidden_width :][:, None, None, None]
    inputs = jnp.concatenate([upper_half.astype(jnp.bfloat16), condition], axis=0)
    framed = frame_cols(extended(inputs, (("gz", 1), ("gx", 2)), 1))
    pre_one = forward_taps(framed, expand_kernel, planes, x_rows) + expand_offset
    act_one = jax.nn.silu(pre_one).astype(jnp.bfloat16)
    pre_two = (
        jnp.einsum("oc,czxy->ozxy", mixing_matrix, act_one, preferred_element_type=jnp.float32)
        + mixing_offset
    )
    act_two = jax.nn.silu(pre_two).astype(jnp.bfloat16)
    act_frame = frame_cols(extended(act_two, (("gz", 1), ("gx", 2)), 1))
    scores = forward_taps(act_frame, project_kernel, planes, x_rows) + project_offset
    log_scale = jnp.tanh(scores[:CH])
    centered = lower_half - scores[CH:]
    recovered = centered * jnp.exp(-log_scale)
    score_grad = jnp.concatenate(
        [cot_lower * centered * (1.0 - log_scale * log_scale), cot_lower], axis=0
    ).astype(jnp.bfloat16)
    recovered, score_grad, lower_grad = (recovered, score_grad, cot_lower * jnp.exp(log_scale))
    score_frame = frame_cols(extended(score_grad, (("gz", 1), ("gx", 2)), 1))
    hidden_grad = backward_taps(score_frame, project_kernel, planes, x_rows)
    mix_grad = (hidden_grad * silu_slope(pre_two)).astype(jnp.bfloat16)
    back_one = jnp.einsum(
        "oc,ozxy->czxy", mixing_matrix, mix_grad, preferred_element_type=jnp.float32
    )
    first_grad = (back_one * silu_slope(pre_one)).astype(jnp.bfloat16)
    first_frame = frame_cols(extended(first_grad, (("gz", 1), ("gx", 2)), 1))
    input_grad = backward_taps(first_frame, expand_kernel, planes, x_rows)
    inner_first, inner_mix, inner_act = (first_grad, mix_grad, act_one)
    expand_term = weight_taps(inner_first, framed)
    mixing_term = jnp.einsum(
        "ozxy,czxy->oc", inner_mix, inner_act, preferred_element_type=jnp.float32
    )
    project_term = weight_taps(score_grad, act_frame)
    offset_term = jnp.concatenate(
        [channel_sums(inner_first), channel_sums(inner_mix), channel_sums(score_grad)]
    )
    expand_sum, mixing_sum, project_sum, offset_sum = lax.psum(
        (expand_term, mixing_term, project_term, offset_term), ("gz", "gx")
    )
    restored = unsqueeze(jnp.concatenate([upper_half, recovered], axis=0))
    field_grad = unsqueeze(jnp.concatenate([cot_upper + input_grad[:CH], lower_grad], axis=0))
    condition_grad = input_grad[CH:]
    factor = 1.0 / math.sqrt(float(planes * x_rows * y_cols))
    return (
        restored,
        field_grad,
        condition_grad,
        expand_sum * factor,
        mixing_sum * factor,
        project_sum * factor,
        offset_sum * factor,
    )


def solution(mesh):
    placed = (
        P(None, "gz", "gx", None),
        P(None, "gz", "gx", None),
        P(None, "gz", "gx", None),
        P(),
        P(),
        P(),
        P(),
    )
    return jax.shard_map(
        per_device,
        mesh=mesh,
        in_specs=placed,
        out_specs=(
            P("gz", "gx", None),
            P("gz", "gx", None),
            P(None, "gz", "gx", None),
            P(),
            P(),
            P(),
            P(),
        ),
        check_vma=False,
    )
```

profile of v0, /device:TPU:1, one launch (start us, length us, event | category | flops | bytes accessed | tf_op | source)
XLA Modules:
  0.0 664.7 jit_solution(13013788002436073114)
XLA Ops:
  7.2 0.7 fusion.552
  8.0 0.7 copy.165
  8.7 4.0 collective-permute-start
  12.8 1.3 collective-permute-start.1
  14.1 1.2 fusion.548
  15.3 1.4 fusion.547
  17.0 0.7 fusion.551
  17.7 0.8 fusion.553
  18.5 0.7 slice.865
  19.3 5.1 collective-permute-start.2
  24.3 2.3 collective-permute-start.3
  26.8 0.6 pad_maximum_fusion.13
  27.5 2.8 collective-permute-done.3
  30.4 0.9 fusion.544
  31.4 0.2 fusion.313
  31.8 0.2 fusion.315
  32.3 0.2 fusion.317
  32.8 0.2 fusion.320
  33.5 0.2 convolution_bitcast_fusion.16
  34.0 0.2 convolution_bitcast_fusion.18
  34.4 0.2 convolution_bitcast_fusion.20
  34.7 0.2 convolution_bitcast_fusion.14
  35.4 0.2 convolution_add_fusion.13
  36.8 0.3 fusion.24
  37.2 0.4 multiply_convert_fusion.1
  37.8 4.5 collective-permute-start.4
  42.4 1.3 collective-permute-start.5
  43.7 0.7 fusion.549
  44.5 4.0 collective-permute-done.5
  48.6 3.6 collective-permute-start.6
  52.2 1.9 collective-permute-start.7
  54.2 5.3 collective-permute-done.7
  59.5 0.4 select_maximum_fusion.4
  64.3 0.6 fusion.309
  65.1 0.6 fusion.541
  65.9 4.3 collective-permute-start.8
  70.1 1.3 collective-permute-start.9
  75.7 0.6 copy.193
  76.4 1.8 reshape.30
  78.4 1.9 collective-permute-start.11
  80.3 4.5 collective-permute-start.10
  85.1 0.5 collective-permute-done.10
  90.4 0.3 fusion.36
  90.9 0.2 fusion.44
  91.4 0.4 convert_reduce_fusion
  91.9 0.8 convolution_bitcast_fusion.34
  92.7 0.3 convert_reduce_fusion.1
  93.2 4.1 collective-permute-start.12
  97.3 1.5 collective-permute-start.13
  102.7 0.7 pad_maximum_fusion.24
  103.6 0.7 copy-done.1
  104.3 278.4 %all-reduce.10.cloned.1.call-done = (f32[64,64]{1,0:T(8,128)}, f32[27,8,64]{2,1,0:T(8,128)}, f32[136]{0:T(256)}) async-done(((f32[64,64]{1,0:T(8,128)}, f32[27,8,64]{2,1,0:T(8,128)}, f32[136]{0:T(256)}), (f32[64,64]{1,0:T(8,128)}, f32[27,8,64]{2,1,0:T(8,128)}, f32[136]{0:T(256)})) %all-reduce.10.cloned.1.call-update) | async-done | bytes 72240 | tf_op jit(solution)/shard_map/psum | solution.py:154
  382.8 1.5 broadcast_multiply_fusion.1
  384.3 1.4 broadcast_multiply_fusion.2
  385.7 1.2 broadcast_multiply_fusion.3
  386.9 1.9 collective-permute-start.15
  388.8 4.5 collective-permute-start.14
  393.4 254.5 %all-reduce.8.cloned.1.call-done = f32[27,64,12]{1,2,0:T(8,128)} async-done(((f32[27,64,12]{1,2,0:T(8,128)}), f32[27,64,12]{1,2,0:T(8,128)}) %all-reduce.8.cloned.1.call-update) | async-done | bytes 82960 | tf_op jit(solution)/shard_map/psum | solution.py:154
  647.9 1.0 broadcast_multiply_fusion
  648.8 0.7 copy.309
  649.5 0.4 select_maximum_fusion
  654.8 0.6 copy.197
  655.4 1.8 reshape.32
  657.3 0.6 copy.308
  (262 shorter events, 27.6 us)
Async XLA Ops:
  7.2 30.4 %copy-start = (bf16[64,64]{1,0:T(8,128)(2,1)S(1)}, bf16[64,64]{1,0:T(8,128)(2,1)}, u32[]{:S(2)}) copy-start(bf16[64,64]{1,0:T(8,128)(2,1)} %param.13) | copy-start | bytes 24580
  7.2 375.6 %all-reduce.10.cloned.1.call-start = ((), (), s32[]{:S(2)}) async-start(), calls=%async_computation.1 | async-start | bytes 288768 | tf_op jit(solution)/shard_map/psum | solution.py:154
  8.7 10.5 %collective-permute-start = (bf16[12,1,4,128]{3,0,2,1:T(8,128)(2,1)S(1)}, bf16[12,1,4,128]{3,0,2,1:T(8,128)(2,1)S(1)}, u32[]{:S(2)}, u32[]{:S(2)}) collective-permute-start(bf16[12,1,4,128]{3,0,2,1:T(8,128)(2,1)S(1)} %get-tuple-element.127), channel_id=1, source_target_pairs={{0,8},{8,16},{16,24},{24,32},{32,40},{40,48},{48,56},{56,64},{64,7... | collective-permute-start | bytes 36872 | tf_op jit(solution)/shard_map/ppermute | solution.py:19
  12.8 6.5 collective-permute-start.1
  16.7 19.4 %copy-start.29 = (bf16[1,64,12]{1,0,2:T(2,128)(2,1)}, bf16[1,64,12]{1,0,2:T(2,128)(2,1)S(1)}, u32[]{:S(2)}) copy-start(bf16[1,64,12]{1,0,2:T(2,128)(2,1)S(1)} %get-tuple-element.85) | copy-start | bytes 4612
  16.7 19.9 %copy-start.35 = (bf16[1,64,12]{1,0,2:T(2,128)(2,1)}, bf16[1,64,12]{1,0,2:T(2,128)(2,1)S(1)}, u32[]{:S(2)}) copy-start(bf16[1,64,12]{1,0,2:T(2,128)(2,1)S(1)} %get-tuple-element.96) | copy-start | bytes 4612
  16.7 20.1 %copy-start.33 = (bf16[1,64,12]{1,0,2:T(2,128)(2,1)}, bf16[1,64,12]{1,0,2:T(2,128)(2,1)S(1)}, u32[]{:S(2)}) copy-start(bf16[1,64,12]{1,0,2:T(2,128)(2,1)S(1)} %get-tuple-element.93) | copy-start | bytes 4612
  16.7 20.4 %copy-start.31 = (bf16[1,64,12]{1,0,2:T(2,128)(2,1)}, bf16[1,64,12]{1,0,2:T(2,128)(2,1)S(1)}, u32[]{:S(2)}) copy-start(bf16[1,64,12]{1,0,2:T(2,128)(2,1)S(1)} %get-tuple-element.78) | copy-start | bytes 4612
  19.3 8.2 %collective-permute-start.2 = (bf16[12,4,1,128]{3,0,2,1:T(8,128)(2,1)S(1)}, bf16[12,4,1,128]{3,0,2,1:T(8,128)(2,1)S(1)}, u32[]{:S(2)}, u32[]{:S(2)}) collective-permute-start(bf16[12,4,1,128]{3,0,2,1:T(8,128)(2,1)S(1)} %get-tuple-element.113), channel_id=1, source_target_pairs={{0,1},{1,2},{2,3},{3,4},{4,5},{5,6},{6,7},{8,9},{9,10},{10,11},{11... | collective-permute-start | bytes 36872 | tf_op jit(solution)/shard_map/ppermute | solution.py:19
  24.3 6.0 collective-permute-start.3
  37.6 6.8 %copy-start.2 = (bf16[27,8,64]{2,1,0:T(8,128)(2,1)S(1)}, bf16[27,8,64]{2,1,0:T(8,128)(2,1)}, u32[]{:S(2)}) copy-start(bf16[27,8,64]{2,1,0:T(8,128)(2,1)} %param.14) | copy-start | bytes 82948
  37.8 6.7 %collective-permute-start.4 = (bf16[64,1,4,128]{3,0,2,1:T(8,128)(2,1)S(1)}, bf16[64,1,4,128]{3,0,2,1:T(8,128)(2,1)S(1)}, u32[]{:S(2)}, u32[]{:S(2)}) collective-permute-start(bf16[64,1,4,128]{3,0,2,1:T(8,128)(2,1)S(1)} %get-tuple-element.76), channel_id=1, source_target_pairs={{0,8},{8,16},{16,24},{24,32},{32,40},{40,48},{48,56},{56,64},{64,7... | collective-permute-start | bytes 196616 | tf_op jit(solution)/shard_map/ppermute | solution.py:19
  42.4 6.2 collective-permute-start.5
  48.6 5.6 collective-permute-start.6
  52.2 7.3 %collective-permute-start.7 = (bf16[64,4,1,128]{3,0,2,1:T(8,128)(2,1)S(1)}, bf16[64,4,1,128]{3,0,2,1:T(8,128)(2,1)S(1)}, u32[]{:S(2)}, u32[]{:S(2)}) collective-permute-start(bf16[64,4,1,128]{3,0,2,1:T(8,128)(2,1)S(1)} %get-tuple-element.53), channel_id=1, source_target_pairs={{1,0},{2,1},{3,2},{4,3},{5,4},{6,5},{7,6},{9,8},{10,9},{11,10},{12... | collective-permute-start | bytes 196616 | tf_op jit(solution)/shard_map/ppermute | solution.py:21
  65.9 12.4 %collective-permute-start.8 = (bf16[8,1,4,128]{3,0,2,1:T(8,128)(2,1)}, bf16[8,1,4,128]{3,0,2,1:T(8,128)(2,1)S(1)}, u32[]{:S(2)}, u32[]{:S(2)}) collective-permute-start(bf16[8,1,4,128]{3,0,2,1:T(8,128)(2,1)} %get-tuple-element.129), channel_id=1, source_target_pairs={{0,8},{8,16},{16,24},{24,32},{32,40},{40,48},{48,56},{56,64},{64,7... | collective-permute-start | bytes 24584 | tf_op jit(solution)/shard_map/ppermute | solution.py:19
  70.1 8.2 %collective-permute-start.9 = (bf16[8,1,4,128]{3,0,2,1:T(8,128)(2,1)}, bf16[8,1,4,128]{3,0,2,1:T(8,128)(2,1)S(1)}, u32[]{:S(2)}, u32[]{:S(2)}) collective-permute-start(bf16[8,1,4,128]{3,0,2,1:T(8,128)(2,1)} %get-tuple-element.130), channel_id=1, source_target_pairs={{8,0},{16,8},{24,16},{32,24},{40,32},{48,40},{56,48},{64,56},{72,6... | collective-permute-start | bytes 24584 | tf_op jit(solution)/shard_map/ppermute | solution.py:21
  72.6 2.9 copy-start.37
  75.5 2.7 copy-start.3
  78.4 6.7 %collective-permute-start.11 = (bf16[8,4,1,128]{3,0,2,1:T(8,128)(2,1)S(1)}, bf16[8,4,1,128]{3,0,2,1:T(8,128)(2,1)S(1)}, u32[]{:S(2)}, u32[]{:S(2)}) collective-permute-start(bf16[8,4,1,128]{3,0,2,1:T(8,128)(2,1)S(1)} %get-tuple-element.121), channel_id=1, source_target_pairs={{1,0},{2,1},{3,2},{4,3},{5,4},{6,5},{7,6},{9,8},{10,9},{11,10},{12... | collective-permute-start | bytes 24584 | tf_op jit(solution)/shard_map/ppermute | solution.py:21
  80.3 5.3 collective-permute-start.10
  91.8 1.2 copy-start.22
  91.8 7.0 %copy-start.28 = (bf16[12,2,4,128]{3,0,2,1:T(8,128)(2,1)S(1)}, bf16[12,2,4,128]{3,0,2,1:T(8,128)(2,1)}, u32[]{:S(2)}) copy-start(bf16[12,2,4,128]{3,0,2,1:T(8,128)(2,1)} %get-tuple-element.144) | copy-start | bytes 73732
  91.8 7.1 %copy-start.21 = (bf16[12,2,4,128]{3,0,2,1:T(8,128)(2,1)S(1)}, bf16[12,2,4,128]{3,0,2,1:T(8,128)(2,1)}, u32[]{:S(2)}) copy-start(bf16[12,2,4,128]{3,0,2,1:T(8,128)(2,1)} %get-tuple-element.70) | copy-start | bytes 73732
  91.8 7.3 %copy-start.20 = (bf16[12,2,4,128]{3,0,2,1:T(8,128)(2,1)S(1)}, bf16[12,2,4,128]{3,0,2,1:T(8,128)(2,1)}, u32[]{:S(2)}) copy-start(bf16[12,2,4,128]{3,0,2,1:T(8,128)(2,1)} %get-tuple-element.69) | copy-start | bytes 73732
  91.9 7.4 %copy-start.15 = (bf16[12,2,4,128]{3,0,2,1:T(8,128)(2,1)S(1)}, bf16[12,2,4,128]{3,0,2,1:T(8,128)(2,1)}, u32[]{:S(2)}) copy-start(bf16[12,2,4,128]{3,0,2,1:T(8,128)(2,1)} %get-tuple-element.125) | copy-start | bytes 73732
  91.9 7.6 %copy-start.19 = (bf16[12,2,4,128]{3,0,2,1:T(8,128)(2,1)S(1)}, bf16[12,2,4,128]{3,0,2,1:T(8,128)(2,1)}, u32[]{:S(2)}) copy-start(bf16[12,2,4,128]{3,0,2,1:T(8,128)(2,1)} %get-tuple-element.68) | copy-start | bytes 73732
  92.6 7.0 %copy-start.18 = (bf16[12,2,4,128]{3,0,2,1:T(8,128)(2,1)S(1)}, bf16[12,2,4,128]{3,0,2,1:T(8,128)(2,1)}, u32[]{:S(2)}) copy-start(bf16[12,2,4,128]{3,0,2,1:T(8,128)(2,1)} %get-tuple-element.67) | copy-start | bytes 73732
  92.7 7.1 %copy-start.27 = (bf16[12,2,4,128]{3,0,2,1:T(8,128)(2,1)S(1)}, bf16[12,2,4,128]{3,0,2,1:T(8,128)(2,1)}, u32[]{:S(2)}) copy-start(bf16[12,2,4,128]{3,0,2,1:T(8,128)(2,1)} %get-tuple-element.107) | copy-start | bytes 73732
  92.7 7.3 %copy-start.17 = (bf16[12,2,4,128]{3,0,2,1:T(8,128)(2,1)S(1)}, bf16[12,2,4,128]{3,0,2,1:T(8,128)(2,1)}, u32[]{:S(2)}) copy-start(bf16[12,2,4,128]{3,0,2,1:T(8,128)(2,1)} %get-tuple-element.66) | copy-start | bytes 73732
  92.7 7.4 %copy-start.16 = (bf16[12,2,4,128]{3,0,2,1:T(8,128)(2,1)S(1)}, bf16[12,2,4,128]{3,0,2,1:T(8,128)(2,1)}, u32[]{:S(2)}) copy-start(bf16[12,2,4,128]{3,0,2,1:T(8,128)(2,1)} %get-tuple-element.65) | copy-start | bytes 73732
  92.7 7.6 %copy-start.26 = (bf16[12,2,4,128]{3,0,2,1:T(8,128)(2,1)S(1)}, bf16[12,2,4,128]{3,0,2,1:T(8,128)(2,1)}, u32[]{:S(2)}) copy-start(bf16[12,2,4,128]{3,0,2,1:T(8,128)(2,1)} %get-tuple-element.145) | copy-start | bytes 73732
  93.0 7.4 %copy-start.14 = (bf16[12,2,4,128]{3,0,2,1:T(8,128)(2,1)S(1)}, bf16[12,2,4,128]{3,0,2,1:T(8,128)(2,1)}, u32[]{:S(2)}) copy-start(bf16[12,2,4,128]{3,0,2,1:T(8,128)(2,1)} %get-tuple-element.64) | copy-start | bytes 73732
  93.0 7.5 %copy-start.13 = (bf16[12,2,4,128]{3,0,2,1:T(8,128)(2,1)S(1)}, bf16[12,2,4,128]{3,0,2,1:T(8,128)(2,1)}, u32[]{:S(2)}) copy-start(bf16[12,2,4,128]{3,0,2,1:T(8,128)(2,1)} %get-tuple-element.63) | copy-start | bytes 73732
  93.0 7.7 %copy-start.6 = (bf16[12,2,4,128]{3,0,2,1:T(8,128)(2,1)S(1)}, bf16[12,2,4,128]{3,0,2,1:T(8,128)(2,1)}, u32[]{:S(2)}) copy-start(bf16[12,2,4,128]{3,0,2,1:T(8,128)(2,1)} %get-tuple-element.126) | copy-start | bytes 73732
  93.0 7.8 %copy-start.12 = (bf16[12,2,4,128]{3,0,2,1:T(8,128)(2,1)S(1)}, bf16[12,2,4,128]{3,0,2,1:T(8,128)(2,1)}, u32[]{:S(2)}) copy-start(bf16[12,2,4,128]{3,0,2,1:T(8,128)(2,1)} %get-tuple-element.62) | copy-start | bytes 73732
  93.1 8.0 %copy-start.11 = (bf16[12,2,4,128]{3,0,2,1:T(8,128)(2,1)S(1)}, bf16[12,2,4,128]{3,0,2,1:T(8,128)(2,1)}, u32[]{:S(2)}) copy-start(bf16[12,2,4,128]{3,0,2,1:T(8,128)(2,1)} %get-tuple-element.61) | copy-start | bytes 73732
  93.2 8.0 %copy-start.25 = (bf16[12,2,4,128]{3,0,2,1:T(8,128)(2,1)S(1)}, bf16[12,2,4,128]{3,0,2,1:T(8,128)(2,1)}, u32[]{:S(2)}) copy-start(bf16[12,2,4,128]{3,0,2,1:T(8,128)(2,1)} %get-tuple-element.106) | copy-start | bytes 73732
  93.2 293.7 %collective-permute-start.12 = (bf16[64,1,4,128]{3,0,2,1:T(8,128)(2,1)S(1)}, bf16[64,1,4,128]{3,0,2,1:T(8,128)(2,1)S(1)}, u32[]{:S(2)}, u32[]{:S(2)}) collective-permute-start(bf16[64,1,4,128]{3,0,2,1:T(8,128)(2,1)S(1)} %get-tuple-element.74), channel_id=1, source_target_pairs={{0,8},{8,16},{16,24},{24,32},{32,40},{40,48},{48,56},{56,64},{64,7... | collective-permute-start | bytes 196616 | tf_op jit(solution)/shard_map/ppermute | solution.py:19
  97.3 289.5 %collective-permute-start.13 = (bf16[64,1,4,128]{3,0,2,1:T(8,128)(2,1)S(1)}, bf16[64,1,4,128]{3,0,2,1:T(8,128)(2,1)S(1)}, u32[]{:S(2)}, u32[]{:S(2)}) collective-permute-start(bf16[64,1,4,128]{3,0,2,1:T(8,128)(2,1)S(1)} %get-tuple-element.75), channel_id=1, source_target_pairs={{8,0},{16,8},{24,16},{32,24},{40,32},{48,40},{56,48},{64,56},{72,6... | collective-permute-start | bytes 196616 | tf_op jit(solution)/shard_map/ppermute | solution.py:21
  99.0 2.4 copy-start.10
  99.1 2.4 copy-start.9
  99.3 2.4 copy-start.24
  99.4 2.4 copy-start.8
  99.6 2.4 copy-start.7
  99.9 2.4 copy-start.5
  100.1 2.3 copy-start.4
  100.2 2.3 copy-start.23
  103.4 544.4 %all-reduce.8.cloned.1.call-start = ((), (), s32[]{:S(2)}) async-start(), calls=%async_computation | async-start | bytes 442368 | tf_op jit(solution)/shard_map/psum | solution.py:154
  103.6 0.7 copy-start.1
  386.9 262.6 %collective-permute-start.15 = (bf16[64,4,1,128]{3,0,2,1:T(8,128)(2,1)S(1)}, bf16[64,4,1,128]{3,0,2,1:T(8,128)(2,1)S(1)}, u32[]{:S(2)}, u32[]{:S(2)}) collective-permute-start(bf16[64,4,1,128]{3,0,2,1:T(8,128)(2,1)S(1)} %get-tuple-element.49), channel_id=1, source_target_pairs={{1,0},{2,1},{3,2},{4,3},{5,4},{6,5},{7,6},{9,8},{10,9},{11,10},{12... | collective-permute-start | bytes 196616 | tf_op jit(solution)/shard_map/ppermute | solution.py:21
  388.8 260.7 %collective-permute-start.14 = (bf16[64,4,1,128]{3,0,2,1:T(8,128)(2,1)S(1)}, bf16[64,4,1,128]{3,0,2,1:T(8,128)(2,1)S(1)}, u32[]{:S(2)}, u32[]{:S(2)}) collective-permute-start(bf16[64,4,1,128]{3,0,2,1:T(8,128)(2,1)S(1)} %get-tuple-element.48), channel_id=1, source_target_pairs={{0,1},{1,2},{2,3},{3,4},{4,5},{5,6},{6,7},{8,9},{9,10},{10,11},{11... | collective-permute-start | bytes 196616 | tf_op jit(solution)/shard_map/ppermute | solution.py:19
  651.4 1.7 copy-start.36
  652.3 1.1 copy-start.34
  653.0 1.0 copy-start.32
  653.2 1.0 copy-start.30
Sparse Core Ops, SparseCore 0:
  103.5 279.2 all-reduce.9
  388.5 259.2 all-reduce.7
where the time goes:
time: 666 us; the launch traced here: 665 us
  waiting for transfers between devices  546 us (82%)
  starting transfers between devices  48.1 us (7%)
  matrix products  31.4 us (5%)
  local copies, waits for them, and re-layouts  15.9 us (2%)
  between operations  15.2 us (2%)
  other arithmetic  8.42 us (1%)
    psum x2, waiting for transfers between devices, per_device(): lax.psum((expand_term, mixing_term, project_term, offset_term), ('gz', 'g...  533 us
    ppermute x8, starting transfers between devices, extended(): lax.ppermute(tail, axis, [(i, (i + 1) % count) for i in range(ends)])  34.7 us
    ppermute x8, starting transfers between devices, extended(): lax.ppermute(head, axis, [((i + 1) % count, i) for i in range(ends)])  13.4 us
  transfers between devices with their start and end apart: 18, of which 6 were waited for; matrix products, arithmetic and copies ran while one was open for 4% of the time, Pallas kernels for 0%

commit v1 on v0

--- a/solution.py
+++ b/solution.py
@@ -152,7 +152,7 @@
         [channel_sums(inner_first), channel_sums(inner_mix), channel_sums(score_grad)]
     )
     expand_sum, mixing_sum, project_sum, offset_sum = lax.psum(
-        (expand_term, mixing_term, project_term, offset_term), ("gz", "gx")
+        lax.psum((expand_term, mixing_term, project_term, offset_term), "gz"), "gx"
     )
     restored = unsqueeze(jnp.concatenate([upper_half, recovered], axis=0))
     field_grad = unsqueeze(jnp.concatenate([cot_upper + input_grad[:CH], lower_grad], axis=0))

time: 666 us -> 1360 us (2.04)
  waiting for transfers between devices: 546 us -> 1250 us
    psum x2 -> x4, waiting for transfers between devices: 533 us -> 1230 us  [the longest x2 1060 us: per_device(): lax.psum((expand_term, mixing_term, project_term, offset_term), 'gz')]
  transfers between devices with their start and end apart: 18 -> 20, of which waited for: 6 -> 8; matrix products, arithmetic and copies ran while one was open for 4% -> 2% of each run, Pallas kernels for 0% -> 0%
where the time goes in v1:
time: 1360 us
  waiting for transfers between devices  1250 us (92%)
  starting transfers between devices  48.9 us (4%)
  matrix products  31.4 us (2%)
  between operations  14.8 us (1%)
  local copies, waits for them, and re-layouts  14.4 us (1%)
    psum x2, waiting for transfers between devices, per_device(): lax.psum((expand_term, mixing_term, project_term, offset_term), 'gz')  1060 us
    psum x2, waiting for transfers between devices, per_device(): lax.psum(lax.psum((expand_term, mixing_term, project_term, offset_term),...  168 us
    ppermute x8, starting transfers between devices, extended(): lax.ppermute(tail, axis, [(i, (i + 1) % count) for i in range(ends)])  35.4 us
  transfers between devices with their start and end apart: 20, of which 8 were waited for; matrix products, arithmetic and copies ran while one was open for 2% of the time, Pallas kernels for 0%

profile of v1, /device:TPU:1, one launch (start us, length us, event | category | flops | bytes accessed | tf_op | source)
XLA Modules:
  0.0 1363.2 jit_solution(4327967251917460005)
XLA Ops:
  7.2 0.7 fusion.552
  8.0 0.7 copy.165
  8.7 4.0 collective-permute-start
  12.8 1.3 collective-permute-start.1
  14.1 1.2 fusion.548
  15.3 1.4 fusion.547
  16.9 0.7 fusion.551
  17.7 0.8 fusion.553
  18.5 0.7 slice.865
  19.2 5.1 collective-permute-start.2
  24.3 2.3 collective-permute-start.3
  26.8 3.4 collective-permute-done.3
  30.6 0.2 fusion.313
  31.0 0.2 fusion.315
  31.5 0.2 fusion.317
  32.0 0.2 fusion.320
  32.7 0.2 convolution_bitcast_fusion.16
  33.2 0.2 convolution_bitcast_fusion.18
  33.6 0.2 convolution_bitcast_fusion.20
  33.9 0.2 convolution_bitcast_fusion.14
  34.6 0.2 convolution_add_fusion.13
  36.0 0.3 fusion.24
  36.3 0.4 multiply_convert_fusion.1
  37.0 4.5 collective-permute-start.4
  41.5 1.3 collective-permute-start.5
  43.0 4.7 collective-permute-done.5
  47.7 3.6 collective-permute-start.6
  51.3 1.9 collective-permute-start.7
  53.3 5.3 collective-permute-done.7
  58.6 0.4 select_maximum_fusion.4
  63.7 0.6 fusion.541
  64.5 4.3 collective-permute-start.8
  68.8 1.3 collective-permute-start.9
  74.4 1.9 collective-permute-start.11
  76.3 4.5 collective-permute-start.10
  81.1 0.5 collective-permute-done.10
  85.0 0.2 convolution_add_fusion.11
  85.4 0.2 convolution_add_fusion.9
  86.4 0.3 fusion.36
  86.9 0.2 fusion.44
  87.4 0.4 convert_reduce_fusion
  87.8 0.8 convolution_bitcast_fusion.34
  88.6 0.3 convert_reduce_fusion.1
  89.1 4.0 collective-permute-start.12
  93.1 1.3 collective-permute-start.13
  98.2 0.7 pad_maximum_fusion.24
  99.1 0.7 copy-done.1
  99.9 1.9 collective-permute-start.15
  101.8 5.4 collective-permute-start.14
  107.2 518.6 %all-reduce.15.cloned.1.call-done = (f32[64,64]{1,0:T(8,128)}, f32[27,8,64]{2,1,0:T(8,128)}, f32[136]{0:T(256)}) async-done(((f32[64,64]{1,0:T(8,128)}, f32[27,8,64]{2,1,0:T(8,128)}, f32[136]{0:T(256)}), (f32[64,64]{1,0:T(8,128)}, f32[27,8,64]{2,1,0:T(8,128)}, f32[136]{0:T(256)})) %all-reduce.15.cloned.1.call-update) | async-done | bytes 72240 | tf_op jit(solution)/shard_map/psum | solution.py:155
  626.2 0.6 copy.193
  626.9 1.8 reshape.30
  628.7 545.4 %all-reduce.11.cloned.1.call-done = f32[27,64,12]{1,2,0:T(8,128)} async-done(((f32[27,64,12]{1,2,0:T(8,128)}), f32[27,64,12]{1,2,0:T(8,128)}) %all-reduce.11.cloned.1.call-update) | async-done | bytes 82960 | tf_op jit(solution)/shard_map/psum | solution.py:155
  1174.1 0.4 select_maximum_fusion
  1179.3 0.6 copy.197
  1179.9 1.8 reshape.32
  1181.8 0.6 copy.308
  1182.4 94.0 %all-reduce.17.cloned.1.call-done = (f32[64,64]{1,0:T(8,128)}, f32[27,8,64]{2,1,0:T(8,128)}, f32[136]{0:T(256)}) async-done(((f32[64,64]{1,0:T(8,128)}, f32[27,8,64]{2,1,0:T(8,128)}, f32[136]{0:T(256)}), (f32[64,64]{1,0:T(8,128)}, f32[27,8,64]{2,1,0:T(8,128)}, f32[136]{0:T(256)})) %all-reduce.17.cloned.1.call-update) | async-done | bytes 72240 | tf_op jit(solution)/shard_map/psum | solution.py:154
  1276.4 1.5 broadcast_multiply_fusion.1
  1278.0 1.4 broadcast_multiply_fusion.2
  1279.3 1.2 broadcast_multiply_fusion.3
  1280.6 74.4 %all-reduce.13.cloned.1.call-done = f32[27,64,12]{1,2,0:T(8,128)} async-done(((f32[27,64,12]{1,2,0:T(8,128)}), f32[27,64,12]{1,2,0:T(8,128)}) %all-reduce.13.cloned.1.call-update) | async-done | bytes 82960 | tf_op jit(solution)/shard_map/psum | solution.py:154
  1355.0 1.0 broadcast_multiply_fusion
  1356.0 0.7 copy.309
  (202 shorter events, 27.5 us)
Async XLA Ops:
  7.2 29.6 %copy-start = (bf16[64,64]{1,0:T(8,128)(2,1)S(1)}, bf16[64,64]{1,0:T(8,128)(2,1)}, u32[]{:S(2)}) copy-start(bf16[64,64]{1,0:T(8,128)(2,1)} %param.13) | copy-start | bytes 24580
  7.2 618.6 %all-reduce.15.cloned.1.call-start = ((), (), s32[]{:S(2)}) async-start(), calls=%async_computation.2 | async-start | bytes 288768 | tf_op jit(solution)/shard_map/psum | solution.py:155
  8.7 10.5 collective-permute-start
  12.8 6.4 collective-permute-start.1
  19.2 7.6 collective-permute-start.2
  24.3 6.0 collective-permute-start.3
  36.7 6.2 copy-start.2
  37.0 6.0 collective-permute-start.4
  41.5 6.2 collective-permute-start.5
  47.7 5.6 collective-permute-start.6
  51.3 7.3 collective-permute-start.7
  64.5 9.8 collective-permute-start.8
  68.8 5.5 collective-permute-start.9
  74.2 9.9 copy-start.3
  74.4 6.7 collective-permute-start.11
  76.3 5.3 collective-permute-start.10
  89.1 10.8 collective-permute-start.12
  93.1 6.8 collective-permute-start.13
  96.7 529.4 %copy-start.4 = (f32[8,8,1,1]{1,0,3,2:T(8,128)S(1)}, f32[8,8,1,1]{1,0,3,2:T(8,128)}, u32[]{:S(2)}) copy-start(f32[8,8,1,1]{1,0,3,2:T(8,128)} %constant.30) | copy-start | bytes 772
  98.9 1075.2 %all-reduce.11.cloned.1.call-start = ((), (), s32[]{:S(2)}) async-start(), calls=%async_computation | async-start | bytes 442368 | tf_op jit(solution)/shard_map/psum | solution.py:155
  99.1 0.7 copy-start.1
  99.8 1176.6 %all-reduce.17.cloned.1.call-start = ((), (), s32[]{:S(2)}) async-start(), calls=%async_computation.3 | async-start | bytes 288768 | tf_op jit(solution)/shard_map/psum | solution.py:154
  99.9 1074.2 %collective-permute-start.15 = (bf16[64,4,1,128]{3,0,2,1:T(8,128)(2,1)S(1)}, bf16[64,4,1,128]{3,0,2,1:T(8,128)(2,1)S(1)}, u32[]{:S(2)}, u32[]{:S(2)}) collective-permute-start(bf16[64,4,1,128]{3,0,2,1:T(8,128)(2,1)S(1)} %get-tuple-element.52), channel_id=1, source_target_pairs={{1,0},{2,1},{3,2},{4,3},{5,4},{6,5},{7,6},{9,8},{10,9},{11,10},{12... | collective-permute-start | bytes 196616 | tf_op jit(solution)/shard_map/ppermute | solution.py:21
  101.8 1072.3 %collective-permute-start.14 = (bf16[64,4,1,128]{3,0,2,1:T(8,128)(2,1)S(1)}, bf16[64,4,1,128]{3,0,2,1:T(8,128)(2,1)S(1)}, u32[]{:S(2)}, u32[]{:S(2)}) collective-permute-start(bf16[64,4,1,128]{3,0,2,1:T(8,128)(2,1)S(1)} %get-tuple-element.51), channel_id=1, source_target_pairs={{0,1},{1,2},{2,3},{3,4},{4,5},{5,6},{6,7},{8,9},{9,10},{10,11},{11... | collective-permute-start | bytes 196616 | tf_op jit(solution)/shard_map/ppermute | solution.py:19
  625.8 729.2 %all-reduce.13.cloned.1.call-start = ((), (), s32[]{:S(2)}) async-start(), calls=%async_computation.1 | async-start | bytes 442368 | tf_op jit(solution)/shard_map/psum | solution.py:154
Sparse Core Ops, SparseCore 0:
  99.0 526.7 all-reduce.14
  628.9 545.0 all-reduce.10
  1177.2 99.1 all-reduce.16
  1279.4 75.5 all-reduce.12
